TPU v7x, 512 devices: a whole 4x4x16 slice. The times are simulated.
512 devices in a mesh: lat: 32 (over z, core), lon: 16 (over x, y).
Axes of the slice: x: 4, y: 4, z: 16, core: 2. Of those that a mesh axis runs over, the one named last changes fastest.
Arguments:
- source: float32 [8, 1024, 2048], P(None, 'lat', 'lon'), may hold values from -6 to 6
- kappa_lon: bfloat16 [8, 1024, 2048], P(None, 'lat', 'lon'), may hold values from 32768 to 262144
- kappa_lat: bfloat16 [8, 1024, 2048], P(None, 'lat', 'lon'), may hold values from 2048 to 16384
- sea_mask: int32 [8, 1024, 2048], P(None, 'lat', 'lon'), may hold values 0 or 1
Outputs:
- analysis: float32 [8, 1024, 2048], P(None, 'lat', 'lon')
All inputs are finite; a program needn't handle non-finite values. No bound on the sum of `sea_mask` on one device may be relied on, other than what follows from the above.
Results may differ from a plain program's by a relative error of at most 0.0003.
Values sent between devices are 32-bit elements; how exact they have to be, the bound alone decides.
No kernel may reach another device: no remote copies, remote signals or barrier semaphores. Data moves between devices by JAX's collectives and lax.ppermute only.
A program may use at most 64 MiB of HBM per device.

v0:
```python
import jax
import jax.numpy as jnp
from jax import lax
from jax.sharding import PartitionSpec as P


def padded(array, sides, width):
    for axis, dim in sides:
        peers, length = (lax.axis_size(axis), array.shape[dim])
        up = [(i, (i + 1) % peers) for i in range(peers)]
        down = [(j, i) for i, j in up]
        last = lax.slice_in_dim(array, length - width, length, axis=dim)
        leading = lax.slice_in_dim(array, 0, width, axis=dim)
        before = lax.ppermute(last, axis, up)
        after = lax.ppermute(leading, axis, down)
        array = jnp.concatenate([before, array, after], axis=dim)
    return array


def earlier(values, stride, axis):
    length = values.shape[axis]
    padding = jnp.zeros_like(lax.slice_in_dim(values, 0, stride, axis=axis))
    return jnp.concatenate([padding, lax.slice_in_dim(values, 0, length - stride, axis=axis)], axis)


def following(values, stride, axis):
    length = values.shape[axis]
    padding = jnp.zeros_like(lax.slice_in_dim(values, 0, stride, axis=axis))
    return jnp.concatenate([lax.slice_in_dim(values, stride, length, axis=axis), padding], axis)


def local_solve(lower_band, upper_band, excess, sources, axis):
    length = lower_band.shape[axis]
    stride = 1
    while stride < length:
        inverse = 1.0 / (excess - lower_band - upper_band)
        left_weight = -lower_band * earlier(inverse, stride, axis)
        right_coefficient = -upper_band * following(inverse, stride, axis)
        new_lower = left_weight * earlier(lower_band, stride, axis)
        new_upper = right_coefficient * following(upper_band, stride, axis)
        excess = (
            excess
            + left_weight * earlier(excess, stride, axis)
            + right_coefficient * following(excess, stride, axis)
        )
        sources = (
            sources
            + left_weight * earlier(sources, stride, axis + 1)
            + right_coefficient * following(sources, stride, axis + 1)
        )
        lower_band, upper_band = (new_lower, new_upper)
        stride = stride * 2
    return sources / (excess - lower_band - upper_band)


def reduced_from(own_terms, next_terms):
    coupling, own_source, own_excess, upper_end = own_terms
    next_particular, next_right, next_deficit = next_terms
    return (
        coupling,
        upper_end * next_right,
        own_excess - upper_end * next_deficit,
        own_source - upper_end * next_particular,
    )


def parallel_cyclic_reduction_update(tridiagonal_system, leading_terms, trailing_terms):
    lower_band, upper_band, excess, sources = tridiagonal_system
    lower_b, upper_b, excess_b, source_b = leading_terms
    lower_a, upper_a, excess_a, source_a = trailing_terms
    left_weight = -lower_band / (excess_b - lower_b - upper_b)
    right_coefficient = -upper_band / (excess_a - lower_a - upper_a)
    return (
        left_weight * lower_b,
        right_coefficient * upper_a,
        excess + left_weight * excess_b + right_coefficient * excess_a,
        sources + left_weight * source_b + right_coefficient * source_a,
    )


def circular_solve(tridiagonal_system):
    devices = tridiagonal_system[0].shape[0]
    stride = 1
    while stride < devices:
        leading_terms = tuple(
            (jnp.roll(ensemble_member, stride, 0) for ensemble_member in tridiagonal_system)
        )
        trailing_terms = tuple(
            (jnp.roll(ensemble_member, -stride, 0) for ensemble_member in tridiagonal_system)
        )
        tridiagonal_system = parallel_cyclic_reduction_update(
            tridiagonal_system, leading_terms, trailing_terms
        )
        stride = stride * 2
    return tridiagonal_system[3] / tridiagonal_system[2]


def gathered_solve(gathered, device_index):
    own_terms = gathered[:4]
    next_terms = tuple((jnp.roll(ensemble_member, -1, 0) for ensemble_member in gathered[4:]))
    interface = circular_solve(reduced_from(own_terms, next_terms))
    devices = interface.shape[0]
    here_value = lax.dynamic_index_in_dim(interface, device_index, 0, keepdims=False)
    before_value = lax.dynamic_index_in_dim(
        interface, (device_index + devices - 1) % devices, 0, keepdims=False
    )
    return (before_value, here_value)


def lon_gathered(own_terms, head_terms):
    gathered = (
        lax.all_gather(own_terms[0][None], "lon", axis=0, tiled=True),
        lax.all_gather(own_terms[1][None], "lon", axis=0, tiled=True),
        lax.all_gather(own_terms[2][None], "lon", axis=0, tiled=True),
        lax.all_gather(own_terms[3][None], "lon", axis=0, tiled=True),
        lax.all_gather(head_terms[0][None], "lon", axis=0, tiled=True),
        lax.all_gather(head_terms[1][None], "lon", axis=0, tiled=True),
        lax.all_gather(head_terms[2][None], "lon", axis=0, tiled=True),
    )
    return gathered_solve(gathered, lax.axis_index("lon"))


def lat_gathered(own_terms, head_terms):
    gathered = (
        lax.all_gather(own_terms[0][None], "lat", axis=0, tiled=True),
        lax.all_gather(own_terms[1][None], "lat", axis=0, tiled=True),
        lax.all_gather(own_terms[2][None], "lat", axis=0, tiled=True),
        lax.all_gather(own_terms[3][None], "lat", axis=0, tiled=True),
        lax.all_gather(head_terms[0][None], "lat", axis=0, tiled=True),
        lax.all_gather(head_terms[1][None], "lat", axis=0, tiled=True),
        lax.all_gather(head_terms[2][None], "lat", axis=0, tiled=True),
    )
    return gathered_solve(gathered, lax.axis_index("lat"))


def line_pass(values, left_face, right_face, axis, reduce_edges):
    length = values.shape[axis]
    position = lax.broadcasted_iota(jnp.int32, values.shape, axis)
    is_first = position == 0
    is_last = position == length - 1
    is_penult = position == length - 2
    lower_band = jnp.where(is_first | is_last, 0.0, -left_face)
    upper_band = jnp.where(is_penult | is_last, 0.0, -right_face)
    excess = 1.0 + jnp.where(is_first, left_face, 0.0) + jnp.where(is_penult, right_face, 0.0)
    sources = jnp.stack(
        [
            jnp.where(is_last, 0.0, values),
            jnp.where(is_first, left_face, 0.0),
            jnp.where(is_penult, right_face, 0.0) + jnp.where(is_last, 1.0, 0.0),
            jnp.where(is_last, 0.0, 1.0),
        ],
        0,
    )
    solved = local_solve(lower_band, upper_band, excess, sources, axis)
    particular, from_left, right_contribution, deficit = (
        solved[0],
        solved[1],
        solved[2],
        solved[3],
    )

    def row_at(ensemble_member, place):
        return lax.index_in_dim(ensemble_member, place, axis, keepdims=False)

    lower_end = -row_at(left_face, length - 1)
    upper_end = -row_at(right_face, length - 1)
    own_terms = (
        lower_end * row_at(from_left, length - 2),
        row_at(values, length - 1) - lower_end * row_at(particular, length - 2),
        1.0 - lower_end * row_at(deficit, length - 2),
        upper_end,
    )
    head_terms = (row_at(particular, 0), row_at(right_contribution, 0), row_at(deficit, 0))
    before_value, here_value = reduce_edges(own_terms, head_terms)
    return (
        particular
        + from_left * jnp.expand_dims(before_value, axis)
        + right_contribution * jnp.expand_dims(here_value, axis)
    )


def shards(source, kappa_lon, kappa_lat, sea_mask):
    wet_cells = sea_mask.astype(jnp.float32)
    lon_kappa = kappa_lon.astype(jnp.float32)
    lat_kappa = kappa_lat.astype(jnp.float32)
    wet_pad, lon_pad, lat_pad = (
        padded(wet_cells, (("lat", 1), ("lon", 2)), 1),
        padded(lon_kappa, (("lat", 1), ("lon", 2)), 1),
        padded(lat_kappa, (("lat", 1), ("lon", 2)), 1),
    )
    lon_wet = wet_pad[:, 1:-1, :]
    lon_faces = lon_pad[:, 1:-1, :-1] * lon_wet[:, :, :-1] * lon_wet[:, :, 1:]
    lon_pass = line_pass(source, lon_faces[:, :, :-1], lon_faces[:, :, 1:], 2, lon_gathered)
    lat_wet = wet_pad[:, :, 1:-1]
    lat_faces = lat_pad[:, :-1, 1:-1] * lat_wet[:, :-1, :] * lat_wet[:, 1:, :]
    device_index = lax.axis_index("lat")
    devices = lax.axis_size("lat")
    position = lax.broadcasted_iota(jnp.int32, lat_faces.shape, 1)
    outer_face = (position == 0) & (device_index == 0) | (position == lat_faces.shape[1] - 1) & (
        device_index == devices - 1
    )
    lat_faces = jnp.where(outer_face, 0.0, lat_faces)
    lat_pass = line_pass(lon_pass, lat_faces[:, :-1, :], lat_faces[:, 1:, :], 1, lat_gathered)
    return wet_cells * 4.0 * jnp.sqrt(jnp.sqrt(lon_kappa * lat_kappa)) * lat_pass


def solution(mesh):
    return jax.shard_map(
        shards,
        mesh=mesh,
        in_specs=(
            P(None, "lat", "lon"),
            P(None, "lat", "lon"),
            P(None, "lat", "lon"),
            P(None, "lat", "lon"),
        ),
        out_specs=P(None, "lat", "lon"),
        check_vma=False,
    )
```

profile of v0, /device:TPU:1, one launch (start us, length us, event | category | flops | bytes accessed | tf_op | source)
XLA Modules:
  0.0 489.6 jit_solution(17990874060258347863)
XLA Ops:
  0.9 3.0 collective-permute-start.7
  4.9 3.8 collective-permute-start.4
  9.7 3.6 collective-permute-start.1
  15.6 6.8 %collective-permute-start.6 = (f32[8,34,1]{2,0,1:T(8,128)S(1)}, f32[8,34,1]{2,0,1:T(8,128)S(1)}, u32[]{:S(2)}, u32[]{:S(2)}) collective-permute-start(f32[8,34,1]{2,0,1:T(8,128)S(1)} %get-tuple-element.145), channel_id=1, source_target_pairs={{1,0},{2,1},{3,2},{4,3},{5,4},{6,5},{7,6},{8,7},{9,8},{10,9},{11,1... | collective-permute-start | bytes 3272 | tf_op jit(solution)/shard_map/ppermute | solution.py:15
  32.0 3.5 collective-permute-done.2
  43.3 26.5 %all-gather.5 = f32[128,32,1]{2,0,1:T(8,128)S(1)} all-gather(f32[8,32,1]{2,0,1:T(8,128)S(1)} %get-tuple-element.263), channel_id=7, replica_groups=mesh['lat'=32,'lon'=16] {'lon'}, dimensions={0}, use_global_device_ids=true | all-gather | bytes 17408 | tf_op jit(solution)/shard_map/all_gather | solution.py:118
  71.2 24.5 %all-gather.6 = f32[128,32,1]{2,0,1:T(8,128)S(1)} all-gather(f32[8,32,1]{2,0,1:T(8,128)S(1)} %bitcast.109), channel_id=8, replica_groups=mesh['lat'=32,'lon'=16] {'lon'}, dimensions={0}, use_global_device_ids=true | all-gather | bytes 17408 | tf_op jit(solution)/shard_map/all_gather | solution.py:117
  97.0 23.1 %all-gather.2 = f32[128,32,1]{2,0,1:T(8,128)S(1)} all-gather(f32[8,32,1]{2,0,1:T(8,128)S(1)} %get-tuple-element.153), channel_id=4, replica_groups=mesh['lat'=32,'lon'=16] {'lon'}, dimensions={0}, use_global_device_ids=true | all-gather | bytes 17408 | tf_op jit(solution)/shard_map/all_gather | solution.py:116
  124.4 22.4 %all-gather.4 = f32[128,32,1]{2,0,1:T(8,128)S(1)} all-gather(f32[8,32,1]{2,0,1:T(8,128)S(1)} %get-tuple-element.140), channel_id=6, replica_groups=mesh['lat'=32,'lon'=16] {'lon'}, dimensions={0}, use_global_device_ids=true | all-gather | bytes 17408 | tf_op jit(solution)/shard_map/all_gather | solution.py:114
  148.0 25.6 %all-gather.1 = f32[128,32,1]{2,0,1:T(8,128)} all-gather(f32[8,32,1]{2,0,1:T(8,128)S(1)} %get-tuple-element.142), channel_id=3, replica_groups=mesh['lat'=32,'lon'=16] {'lon'}, dimensions={0}, use_global_device_ids=true | all-gather | bytes 17408 | tf_op jit(solution)/shard_map/all_gather | solution.py:115
  173.7 2.6 copy.161
  178.0 2.9 copy.162
  180.9 24.8 %all-gather = f32[128,32,1]{2,0,1:T(8,128)S(1)} all-gather(f32[8,32,1]{2,0,1:T(8,128)S(1)} %get-tuple-element.143), channel_id=2, replica_groups=mesh['lat'=32,'lon'=16] {'lon'}, dimensions={0}, use_global_device_ids=true | all-gather | bytes 17408 | tf_op jit(solution)/shard_map/all_gather | solution.py:113
  209.7 29.7 %all-gather.3 = f32[128,32,1]{2,0,1:T(8,128)S(1)} all-gather(f32[8,32,1]{2,0,1:T(8,128)} %get-tuple-element.141), channel_id=5, replica_groups=mesh['lat'=32,'lon'=16] {'lon'}, dimensions={0}, use_global_device_ids=true | all-gather | bytes 17408 | tf_op jit(solution)/shard_map/all_gather | solution.py:112
  239.4 2.2 fusion.84
  243.1 2.3 copy.169
  249.3 2.3 copy.172
  256.6 61.3 %all-gather.12 = f32[256,1,128]{2,0,1:T(8,128)S(1)} all-gather(f32[8,1,128]{2,0,1:T(8,128)S(1)} %get-tuple-element.238), channel_id=14, replica_groups=mesh['lat'=32,'lon'=16] {'lat'}, dimensions={0}, use_global_device_ids=true | all-gather | bytes 135168 | tf_op jit(solution)/shard_map/all_gather | solution.py:131
  317.9 27.5 %all-gather.13 = f32[256,1,128]{2,0,1:T(8,128)S(1)} all-gather(f32[8,1,128]{2,0,1:T(8,128)S(1)} %slice.1405), channel_id=15, replica_groups=mesh['lat'=32,'lon'=16] {'lat'}, dimensions={0}, use_global_device_ids=true | all-gather | bytes 135168 | tf_op jit(solution)/shard_map/all_gather | solution.py:130
  345.4 28.8 %all-gather.9 = f32[256,1,128]{2,0,1:T(8,128)S(1)} all-gather(f32[8,1,128]{2,0,1:T(8,128)S(1)} %get-tuple-element.152), channel_id=11, replica_groups=mesh['lat'=32,'lon'=16] {'lat'}, dimensions={0}, use_global_device_ids=true | all-gather | bytes 135168 | tf_op jit(solution)/shard_map/all_gather | solution.py:129
  374.2 27.5 %all-gather.11 = f32[256,1,128]{2,0,1:T(8,128)S(1)} all-gather(f32[8,1,128]{2,0,1:T(8,128)S(1)} %get-tuple-element.148), channel_id=13, replica_groups=mesh['lat'=32,'lon'=16] {'lat'}, dimensions={0}, use_global_device_ids=true | all-gather | bytes 135168 | tf_op jit(solution)/shard_map/all_gather | solution.py:127
  401.6 28.8 %all-gather.8 = f32[256,1,128]{2,0,1:T(8,128)S(1)} all-gather(f32[8,1,128]{2,0,1:T(8,128)S(1)} %get-tuple-element.150), channel_id=10, replica_groups=mesh['lat'=32,'lon'=16] {'lat'}, dimensions={0}, use_global_device_ids=true | all-gather | bytes 135168 | tf_op jit(solution)/shard_map/all_gather | solution.py:128
  430.4 27.4 %all-gather.7 = f32[256,1,128]{2,0,1:T(8,128)S(1)} all-gather(f32[8,1,128]{2,0,1:T(8,128)S(1)} %get-tuple-element.151), channel_id=9, replica_groups=mesh['lat'=32,'lon'=16] {'lat'}, dimensions={0}, use_global_device_ids=true | all-gather | bytes 135168 | tf_op jit(solution)/shard_map/all_gather | solution.py:126
  457.9 28.8 %all-gather.10 = f32[256,1,128]{2,0,1:T(8,128)S(1)} all-gather(f32[8,1,128]{2,0,1:T(8,128)S(1)} %get-tuple-element.149), channel_id=12, replica_groups=mesh['lat'=32,'lon'=16] {'lat'}, dimensions={0}, use_global_device_ids=true | all-gather | bytes 135168 | tf_op jit(solution)/shard_map/all_gather | solution.py:125
  (295 shorter events, 48.2 us)
Async XLA Ops:
  0.9 25.6 %collective-permute-start.7 = (f32[8,1,128]{2,0,1:T(8,128)S(1)}, f32[8,1,128]{2,0,1:T(8,128)S(1)}, u32[]{:S(2)}, u32[]{:S(2)}) collective-permute-start(f32[8,1,128]{2,0,1:T(8,128)S(1)} %slice.1338), channel_id=1, source_target_pairs={{0,16},{16,32},{32,48},{48,64},{64,80},{80,96},{96,112},{112,128},... | collective-permute-start | bytes 12296 | tf_op jit(solution)/shard_map/ppermute | solution.py:14
  4.9 10.6 %collective-permute-start.3 = (f32[8,1,128]{2,0,1:T(8,128)S(1)}, f32[8,1,128]{2,0,1:T(8,128)S(1)}, u32[]{:S(2)}, u32[]{:S(2)}) collective-permute-start(f32[8,1,128]{2,0,1:T(8,128)S(1)} %get-tuple-element.297), channel_id=1, source_target_pairs={{0,16},{16,32},{32,48},{48,64},{64,80},{80,96},{96,112},{112,128},... | collective-permute-start | bytes 12296 | tf_op jit(solution)/shard_map/ppermute | solution.py:14
  4.9 10.6 %collective-permute-start.4 = (f32[8,1,128]{2,0,1:T(8,128)S(1)}, f32[8,1,128]{2,0,1:T(8,128)S(1)}, u32[]{:S(2)}, u32[]{:S(2)}) collective-permute-start(f32[8,1,128]{2,0,1:T(8,128)S(1)} %get-tuple-element.296), channel_id=1, source_target_pairs={{16,0},{32,16},{48,32},{64,48},{80,64},{96,80},{112,96},{128,112},... | collective-permute-start | bytes 12296 | tf_op jit(solution)/shard_map/ppermute | solution.py:15
  9.7 14.7 %collective-permute-start.1 = (f32[8,1,128]{2,0,1:T(8,128)S(1)}, f32[8,1,128]{2,0,1:T(8,128)S(1)}, u32[]{:S(2)}, u32[]{:S(2)}) collective-permute-start(f32[8,1,128]{2,0,1:T(8,128)S(1)} %get-tuple-element.295), channel_id=1, source_target_pairs={{16,0},{32,16},{48,32},{64,48},{80,64},{96,80},{112,96},{128,112},... | collective-permute-start | bytes 12296 | tf_op jit(solution)/shard_map/ppermute | solution.py:15
  13.3 11.2 %collective-permute-start = (f32[8,1,128]{2,0,1:T(8,128)S(1)}, f32[8,1,128]{2,0,1:T(8,128)S(1)}, u32[]{:S(2)}, u32[]{:S(2)}) collective-permute-start(f32[8,1,128]{2,0,1:T(8,128)S(1)} %get-tuple-element.294), channel_id=1, source_target_pairs={{0,16},{16,32},{32,48},{48,64},{64,80},{80,96},{96,112},{112,128},... | collective-permute-start | bytes 12296 | tf_op jit(solution)/shard_map/ppermute | solution.py:14
  15.6 15.5 %collective-permute-start.6 = (f32[8,34,1]{2,0,1:T(8,128)S(1)}, f32[8,34,1]{2,0,1:T(8,128)S(1)}, u32[]{:S(2)}, u32[]{:S(2)}) collective-permute-start(f32[8,34,1]{2,0,1:T(8,128)S(1)} %get-tuple-element.145), channel_id=1, source_target_pairs={{1,0},{2,1},{3,2},{4,3},{5,4},{6,5},{7,6},{8,7},{9,8},{10,9},{11,1... | collective-permute-start | bytes 3272 | tf_op jit(solution)/shard_map/ppermute | solution.py:15
  22.5 9.5 %collective-permute-start.5 = (f32[8,34,1]{2,0,1:T(8,128)S(1)}, f32[8,34,1]{2,0,1:T(8,128)S(1)}, u32[]{:S(2)}, u32[]{:S(2)}) collective-permute-start(f32[8,34,1]{2,0,1:T(8,128)S(1)} %get-tuple-element.144), channel_id=1, source_target_pairs={{0,1},{1,2},{2,3},{3,4},{4,5},{5,6},{6,7},{7,8},{8,9},{9,10},{10,1... | collective-permute-start | bytes 3272 | tf_op jit(solution)/shard_map/ppermute | solution.py:14
  24.5 10.9 %collective-permute-start.2 = (f32[8,34,1]{2,0,1:T(8,128)S(1)}, f32[8,34,1]{2,0,1:T(8,128)S(1)}, u32[]{:S(2)}, u32[]{:S(2)}) collective-permute-start(f32[8,34,1]{2,0,1:T(8,128)S(1)} %pad_maximum_fusion.11), channel_id=1, source_target_pairs={{0,1},{1,2},{2,3},{3,4},{4,5},{5,6},{6,7},{7,8},{8,9},{9,10},{10,1... | collective-permute-start | bytes 3272 | tf_op jit(solution)/shard_map/ppermute | solution.py:14
  42.4 28.8 %copy-start.4 = (f32[8,32,128]{2,0,1:T(8,128)}, f32[8,32,128]{2,0,1:T(8,128)S(1)}, u32[]{:S(2)}) copy-start(f32[8,32,128]{2,0,1:T(8,128)S(1)} %get-tuple-element.121) | copy-start | bytes 393220
  69.8 1.4 copy-start
  95.7 1.4 copy-start.1
  120.1 2.2 slice-start
  120.8 2.3 slice-start.1
  148.0 28.3 %slice-start.2 = ((f32[128,32,1]{2,0,1:T(8,128)}), f32[8,32,1]{2,0,1:T(8,128)S(1)}, s32[]{:S(2)}) async-start(f32[128,32,1]{2,0,1:T(8,128)} %copy-done.1), calls=%async_computation.2 | async-start | bytes 262144 | tf_op jit(solution)/shard_map/jit(_roll_static)/slice | solution.py:100
  148.0 28.4 %slice-start.3 = ((f32[128,32,1]{2,0,1:T(8,128)}), f32[120,32,1]{2,0,1:T(8,128)S(1)}, s32[]{:S(2)}) async-start(f32[128,32,1]{2,0,1:T(8,128)} %copy-done.1), calls=%async_computation.3 | async-start | bytes 3932160 | tf_op jit(solution)/shard_map/jit(_roll_static)/slice | solution.py:100
  173.7 4.2 copy-start.10
  248.2 3.4 copy-start.2
  248.2 3.4 copy-start.18
  248.2 3.4 copy-start.21
  248.2 3.4 copy-start.22
  248.2 3.4 copy-start.23
  248.2 3.4 copy-start.24
  253.5 1.0 copy-start.6
  254.6 1.0 copy-start.17
  (15 other events, 13.5 us)
where the time goes:
time: 490 us
  blocking collectives  407 us (83%)
  local copies, waits for them, and re-layouts  38.8 us (8%)
  starting transfers between devices  21.2 us (4%)
  other arithmetic  17.1 us (3%)
    all_gather x1, blocking collectives, lat_gathered(): lax.all_gather(head_terms[2][None], 'lat', axis=0, tiled=True)  61.3 us
    all_gather x1, blocking collectives, lon_gathered(): lax.all_gather(own_terms[0][None], 'lon', axis=0, tiled=True)  29.7 us
    all_gather x1, blocking collectives, lat_gathered(): lax.all_gather(head_terms[0][None], 'lat', axis=0, tiled=True)  28.8 us
    all_gather x1, blocking collectives, lat_gathered(): lax.all_gather(own_terms[0][None], 'lat', axis=0, tiled=True)  28.8 us
    all_gather x1, blocking collectives, lat_gathered(): lax.all_gather(own_terms[3][None], 'lat', axis=0, tiled=True)  28.8 us
    all_gather x1, blocking collectives, lat_gathered(): lax.all_gather(own_terms[2][None], 'lat', axis=0, tiled=True)  27.5 us
    all_gather x1, blocking collectives, lat_gathered(): lax.all_gather(head_terms[1][None], 'lat', axis=0, tiled=True)  27.5 us
    all_gather x1, blocking collectives, lat_gathered(): lax.all_gather(own_terms[1][None], 'lat', axis=0, tiled=True)  27.4 us
  transfers between devices with their start and end apart: 8, of which 2 were waited for; matrix products, arithmetic and copies ran while one was open for 2% of the time, Pallas kernels for 0%

commit v1 on v0

--- a/solution.py
+++ b/solution.py
@@ -127,7 +127,10 @@
         lax.all_gather(own_terms[2][None], "lat", axis=0, tiled=True),
         lax.all_gather(own_terms[3][None], "lat", axis=0, tiled=True),
         lax.all_gather(head_terms[0][None], "lat", axis=0, tiled=True),
-        lax.all_gather(head_terms[1][None], "lat", axis=0, tiled=True),
+        jnp.concatenate(
+            lax.all_to_all(jnp.stack([head_terms[1][None]] * lax.axis_size("lat")), "lat", 0, 0),
+            axis=0,
+        ),
         lax.all_gather(head_terms[2][None], "lat", axis=0, tiled=True),
     )
     return gathered_solve(gathered, lax.axis_index("lat"))

time: 490 us -> 476 us (0.971)
  blocking collectives: 407 us -> 385 us
  starting transfers between devices: 21.2 us -> 27.5 us
    all_gather x1 -> x0, blocking collectives: 27.5 us -> none  [lat_gathered(): lax.all_gather(head_terms[1][None], 'lat', axis=0, tiled=True)]
    all_to_all x0 -> x1, starting transfers between devices: none -> 6.33 us  [lat_gathered(): lax.all_to_all(jnp.stack([head_terms[1][None]] * lax.axis_size('lat')), '...]
  transfers between devices with their start and end apart: 8 -> 9, of which waited for: 2 -> 2; matrix products, arithmetic and copies ran while one was open for 2% -> 2% of each run, Pallas kernels for 0% -> 0%
where the time goes in v1:
time: 476 us; the launch traced here: 475 us
  blocking collectives  385 us (81%)
  local copies, waits for them, and re-layouts  39.5 us (8%)
  starting transfers between devices  27.5 us (6%)
  other arithmetic  17.1 us (4%)
    all_gather x1, blocking collectives, lat_gathered(): lax.all_gather(head_terms[2][None], 'lat', axis=0, tiled=True)  61.4 us
    all_gather x1, blocking collectives, lat_gathered(): lax.all_gather(head_terms[0][None], 'lat', axis=0, tiled=True)  33.2 us
    all_gather x1, blocking collectives, lon_gathered(): lax.all_gather(own_terms[0][None], 'lon', axis=0, tiled=True)  29.7 us
    all_gather x1, blocking collectives, lat_gathered(): lax.all_gather(own_terms[1][None], 'lat', axis=0, tiled=True)  29.5 us
    all_gather x1, blocking collectives, lat_gathered(): lax.all_gather(own_terms[3][None], 'lat', axis=0, tiled=True)  28.8 us
    all_gather x1, blocking collectives, lat_gathered(): lax.all_gather(own_terms[0][None], 'lat', axis=0, tiled=True)  27.9 us
    all_gather x1, blocking collectives, lat_gathered(): lax.all_gather(own_terms[2][None], 'lat', axis=0, tiled=True)  27.5 us
    all_gather x1, blocking collectives, lon_gathered(): lax.all_gather(head_terms[2][None], 'lon', axis=0, tiled=True)  26.5 us
  transfers between devices with their start and end apart: 9, of which 2 were waited for; matrix products, arithmetic and copies ran while one was open for 2% of the time, Pallas kernels for 0%

profile of v1, /device:TPU:1, one launch (start us, length us, event | category | flops | bytes accessed | tf_op | source)
XLA Modules:
  0.0 474.9 jit_solution(16520644863435975400)
XLA Ops:
  0.9 3.0 collective-permute-start.7
  4.9 3.8 collective-permute-start.4
  9.7 3.6 collective-permute-start.1
  15.6 6.8 %collective-permute-start.6 = (f32[8,34,1]{2,0,1:T(8,128)S(1)}, f32[8,34,1]{2,0,1:T(8,128)S(1)}, u32[]{:S(2)}, u32[]{:S(2)}) collective-permute-start(f32[8,34,1]{2,0,1:T(8,128)S(1)} %get-tuple-element.145), channel_id=1, source_target_pairs={{1,0},{2,1},{3,2},{4,3},{5,4},{6,5},{7,6},{8,7},{9,8},{10,9},{11,1... | collective-permute-start | bytes 3272 | tf_op jit(solution)/shard_map/ppermute | solution.py:15
  31.9 3.5 collective-permute-done.2
  43.2 26.5 %all-gather.5 = f32[128,32,1]{2,0,1:T(8,128)S(1)} all-gather(f32[8,32,1]{2,0,1:T(8,128)S(1)} %get-tuple-element.263), channel_id=7, replica_groups=mesh['lat'=32,'lon'=16] {'lon'}, dimensions={0}, use_global_device_ids=true | all-gather | bytes 17408 | tf_op jit(solution)/shard_map/all_gather | solution.py:118
  71.1 24.5 %all-gather.6 = f32[128,32,1]{2,0,1:T(8,128)S(1)} all-gather(f32[8,32,1]{2,0,1:T(8,128)S(1)} %bitcast.111), channel_id=8, replica_groups=mesh['lat'=32,'lon'=16] {'lon'}, dimensions={0}, use_global_device_ids=true | all-gather | bytes 17408 | tf_op jit(solution)/shard_map/all_gather | solution.py:117
  97.0 23.1 %all-gather.2 = f32[128,32,1]{2,0,1:T(8,128)S(1)} all-gather(f32[8,32,1]{2,0,1:T(8,128)S(1)} %get-tuple-element.153), channel_id=4, replica_groups=mesh['lat'=32,'lon'=16] {'lon'}, dimensions={0}, use_global_device_ids=true | all-gather | bytes 17408 | tf_op jit(solution)/shard_map/all_gather | solution.py:116
  124.4 22.4 %all-gather.4 = f32[128,32,1]{2,0,1:T(8,128)S(1)} all-gather(f32[8,32,1]{2,0,1:T(8,128)S(1)} %get-tuple-element.140), channel_id=6, replica_groups=mesh['lat'=32,'lon'=16] {'lon'}, dimensions={0}, use_global_device_ids=true | all-gather | bytes 17408 | tf_op jit(solution)/shard_map/all_gather | solution.py:114
  148.0 25.6 %all-gather.1 = f32[128,32,1]{2,0,1:T(8,128)} all-gather(f32[8,32,1]{2,0,1:T(8,128)S(1)} %get-tuple-element.142), channel_id=3, replica_groups=mesh['lat'=32,'lon'=16] {'lon'}, dimensions={0}, use_global_device_ids=true | all-gather | bytes 17408 | tf_op jit(solution)/shard_map/all_gather | solution.py:115
  173.6 2.6 copy.157
  178.0 2.9 copy.158
  180.9 24.9 %all-gather = f32[128,32,1]{2,0,1:T(8,128)S(1)} all-gather(f32[8,32,1]{2,0,1:T(8,128)S(1)} %get-tuple-element.143), channel_id=2, replica_groups=mesh['lat'=32,'lon'=16] {'lon'}, dimensions={0}, use_global_device_ids=true | all-gather | bytes 17408 | tf_op jit(solution)/shard_map/all_gather | solution.py:113
  209.8 29.7 %all-gather.3 = f32[128,32,1]{2,0,1:T(8,128)S(1)} all-gather(f32[8,32,1]{2,0,1:T(8,128)} %get-tuple-element.141), channel_id=5, replica_groups=mesh['lat'=32,'lon'=16] {'lon'}, dimensions={0}, use_global_device_ids=true | all-gather | bytes 17408 | tf_op jit(solution)/shard_map/all_gather | solution.py:112
  239.4 2.2 fusion.84
  243.2 2.3 copy.165
  249.4 2.3 copy.168
  256.6 61.4 %all-gather.12 = f32[256,1,128]{2,0,1:T(8,128)S(1)} all-gather(f32[8,1,128]{2,0,1:T(8,128)S(1)} %get-tuple-element.238), channel_id=14, replica_groups=mesh['lat'=32,'lon'=16] {'lat'}, dimensions={0}, use_global_device_ids=true | all-gather | bytes 135168 | tf_op jit(solution)/shard_map/all_gather | solution.py:134
  318.0 27.5 %all-gather.11 = f32[256,1,128]{2,0,1:T(8,128)S(1)} all-gather(f32[8,1,128]{2,0,1:T(8,128)S(1)} %get-tuple-element.148), channel_id=13, replica_groups=mesh['lat'=32,'lon'=16] {'lat'}, dimensions={0}, use_global_device_ids=true | all-gather | bytes 135168 | tf_op jit(solution)/shard_map/all_gather | solution.py:127
  345.5 28.8 %all-gather.8 = f32[256,1,128]{2,0,1:T(8,128)S(1)} all-gather(f32[8,1,128]{2,0,1:T(8,128)S(1)} %get-tuple-element.150), channel_id=10, replica_groups=mesh['lat'=32,'lon'=16] {'lat'}, dimensions={0}, use_global_device_ids=true | all-gather | bytes 135168 | tf_op jit(solution)/shard_map/all_gather | solution.py:128
  374.9 6.3 %all-to-all-start = ((f32[32,1,8,128]{3,2,1,0:T(8,128)}), f32[32,1,8,128]{3,2,1,0:T(8,128)S(1)}, u32[]{:S(2)}, u32[]{:S(2)}) async-start(f32[32,1,8,128]{3,2,1,0:T(8,128)} %stack.40), calls=%async_computation | async-start | bytes 262144 | tf_op jit(solution)/shard_map/all_to_all | solution.py:131
  381.2 33.2 %all-gather.9 = f32[256,1,128]{2,0,1:T(8,128)S(1)} all-gather(f32[8,1,128]{2,0,1:T(8,128)S(1)} %get-tuple-element.152), channel_id=11, replica_groups=mesh['lat'=32,'lon'=16] {'lat'}, dimensions={0}, use_global_device_ids=true | all-gather | bytes 135168 | tf_op jit(solution)/shard_map/all_gather | solution.py:129
  414.4 27.9 %all-gather.10 = f32[256,1,128]{2,0,1:T(8,128)S(1)} all-gather(f32[8,1,128]{2,0,1:T(8,128)S(1)} %get-tuple-element.149), channel_id=12, replica_groups=mesh['lat'=32,'lon'=16] {'lat'}, dimensions={0}, use_global_device_ids=true | all-gather | bytes 135168 | tf_op jit(solution)/shard_map/all_gather | solution.py:125
  442.4 29.5 %all-gather.7 = f32[256,1,128]{2,0,1:T(8,128)S(1)} all-gather(f32[8,1,128]{2,0,1:T(8,128)S(1)} %get-tuple-element.151), channel_id=9, replica_groups=mesh['lat'=32,'lon'=16] {'lat'}, dimensions={0}, use_global_device_ids=true | all-gather | bytes 135168 | tf_op jit(solution)/shard_map/all_gather | solution.py:126
  (297 shorter events, 48.9 us)
Async XLA Ops:
  0.9 25.5 %collective-permute-start.7 = (f32[8,1,128]{2,0,1:T(8,128)S(1)}, f32[8,1,128]{2,0,1:T(8,128)S(1)}, u32[]{:S(2)}, u32[]{:S(2)}) collective-permute-start(f32[8,1,128]{2,0,1:T(8,128)S(1)} %slice.1344), channel_id=1, source_target_pairs={{0,16},{16,32},{32,48},{48,64},{64,80},{80,96},{96,112},{112,128},... | collective-permute-start | bytes 12296 | tf_op jit(solution)/shard_map/ppermute | solution.py:14
  4.9 10.5 %collective-permute-start.3 = (f32[8,1,128]{2,0,1:T(8,128)S(1)}, f32[8,1,128]{2,0,1:T(8,128)S(1)}, u32[]{:S(2)}, u32[]{:S(2)}) collective-permute-start(f32[8,1,128]{2,0,1:T(8,128)S(1)} %get-tuple-element.297), channel_id=1, source_target_pairs={{0,16},{16,32},{32,48},{48,64},{64,80},{80,96},{96,112},{112,128},... | collective-permute-start | bytes 12296 | tf_op jit(solution)/shard_map/ppermute | solution.py:14
  4.9 10.5 %collective-permute-start.4 = (f32[8,1,128]{2,0,1:T(8,128)S(1)}, f32[8,1,128]{2,0,1:T(8,128)S(1)}, u32[]{:S(2)}, u32[]{:S(2)}) collective-permute-start(f32[8,1,128]{2,0,1:T(8,128)S(1)} %get-tuple-element.296), channel_id=1, source_target_pairs={{16,0},{32,16},{48,32},{64,48},{80,64},{96,80},{112,96},{128,112},... | collective-permute-start | bytes 12296 | tf_op jit(solution)/shard_map/ppermute | solution.py:15
  9.7 14.7 %collective-permute-start.1 = (f32[8,1,128]{2,0,1:T(8,128)S(1)}, f32[8,1,128]{2,0,1:T(8,128)S(1)}, u32[]{:S(2)}, u32[]{:S(2)}) collective-permute-start(f32[8,1,128]{2,0,1:T(8,128)S(1)} %get-tuple-element.295), channel_id=1, source_target_pairs={{16,0},{32,16},{48,32},{64,48},{80,64},{96,80},{112,96},{128,112},... | collective-permute-start | bytes 12296 | tf_op jit(solution)/shard_map/ppermute | solution.py:15
  13.3 11.1 %collective-permute-start = (f32[8,1,128]{2,0,1:T(8,128)S(1)}, f32[8,1,128]{2,0,1:T(8,128)S(1)}, u32[]{:S(2)}, u32[]{:S(2)}) collective-permute-start(f32[8,1,128]{2,0,1:T(8,128)S(1)} %get-tuple-element.294), channel_id=1, source_target_pairs={{0,16},{16,32},{32,48},{48,64},{64,80},{80,96},{96,112},{112,128},... | collective-permute-start | bytes 12296 | tf_op jit(solution)/shard_map/ppermute | solution.py:14
  15.6 15.5 %collective-permute-start.6 = (f32[8,34,1]{2,0,1:T(8,128)S(1)}, f32[8,34,1]{2,0,1:T(8,128)S(1)}, u32[]{:S(2)}, u32[]{:S(2)}) collective-permute-start(f32[8,34,1]{2,0,1:T(8,128)S(1)} %get-tuple-element.145), channel_id=1, source_target_pairs={{1,0},{2,1},{3,2},{4,3},{5,4},{6,5},{7,6},{8,7},{9,8},{10,9},{11,1... | collective-permute-start | bytes 3272 | tf_op jit(solution)/shard_map/ppermute | solution.py:15
  22.4 9.5 %collective-permute-start.5 = (f32[8,34,1]{2,0,1:T(8,128)S(1)}, f32[8,34,1]{2,0,1:T(8,128)S(1)}, u32[]{:S(2)}, u32[]{:S(2)}) collective-permute-start(f32[8,34,1]{2,0,1:T(8,128)S(1)} %get-tuple-element.144), channel_id=1, source_target_pairs={{0,1},{1,2},{2,3},{3,4},{4,5},{5,6},{6,7},{7,8},{8,9},{9,10},{10,1... | collective-permute-start | bytes 3272 | tf_op jit(solution)/shard_map/ppermute | solution.py:14
  24.5 10.9 %collective-permute-start.2 = (f32[8,34,1]{2,0,1:T(8,128)S(1)}, f32[8,34,1]{2,0,1:T(8,128)S(1)}, u32[]{:S(2)}, u32[]{:S(2)}) collective-permute-start(f32[8,34,1]{2,0,1:T(8,128)S(1)} %pad_maximum_fusion.11), channel_id=1, source_target_pairs={{0,1},{1,2},{2,3},{3,4},{4,5},{5,6},{6,7},{7,8},{8,9},{9,10},{10,1... | collective-permute-start | bytes 3272 | tf_op jit(solution)/shard_map/ppermute | solution.py:14
  42.3 28.8 %copy-start.4 = (f32[8,32,128]{2,0,1:T(8,128)}, f32[8,32,128]{2,0,1:T(8,128)S(1)}, u32[]{:S(2)}) copy-start(f32[8,32,128]{2,0,1:T(8,128)S(1)} %get-tuple-element.121) | copy-start | bytes 393220
  69.7 1.4 copy-start
  95.6 1.4 copy-start.1
  120.0 2.2 slice-start
  120.7 2.3 slice-start.1
  148.0 28.3 %slice-start.2 = ((f32[128,32,1]{2,0,1:T(8,128)}), f32[8,32,1]{2,0,1:T(8,128)S(1)}, s32[]{:S(2)}) async-start(f32[128,32,1]{2,0,1:T(8,128)} %copy-done.1), calls=%async_computation.3 | async-start | bytes 262144 | tf_op jit(solution)/shard_map/jit(_roll_static)/slice | solution.py:100
  148.0 28.4 %slice-start.3 = ((f32[128,32,1]{2,0,1:T(8,128)}), f32[120,32,1]{2,0,1:T(8,128)S(1)}, s32[]{:S(2)}) async-start(f32[128,32,1]{2,0,1:T(8,128)} %copy-done.1), calls=%async_computation.4 | async-start | bytes 3932160 | tf_op jit(solution)/shard_map/jit(_roll_static)/slice | solution.py:100
  173.6 4.2 copy-start.10
  248.3 3.4 copy-start.2
  248.3 3.4 copy-start.18
  248.3 3.4 copy-start.21
  248.3 3.4 copy-start.22
  248.3 3.4 copy-start.23
  248.3 3.4 copy-start.24
  254.7 1.0 copy-start.17
  374.9 97.0 %all-to-all-start = ((f32[32,1,8,128]{3,2,1,0:T(8,128)}), f32[32,1,8,128]{3,2,1,0:T(8,128)S(1)}, u32[]{:S(2)}, u32[]{:S(2)}) async-start(f32[32,1,8,128]{3,2,1,0:T(8,128)} %stack.40), calls=%async_computation | async-start | bytes 262144 | tf_op jit(solution)/shard_map/all_to_all | solution.py:131
  (16 other events, 14.5 us)
